TPU v7x, 128 devices: a whole 4x4x4 slice. The times are simulated.
128 devices in a mesh: aux: 4 (over x), row: 32 (over z, y, core).
Axes of the slice: x: 4, y: 4, z: 4, core: 2. Of those that a mesh axis runs over, the one named last changes fastest.
Arguments:
- b_tiles: bfloat16 [4, 32768, 2048], P('aux', 'row'), may hold values from -0.125 to 0.125
- occ_coeff: bfloat16 [32768, 256], P('row'), may hold values from -3 to 3
- tile_blocks: int32 [256, 16], P('row'), may hold values from 0 to 255, as said below
- screen_mask: int32 [256, 16], P('row'), may hold values from 0 to 1, as said below
Outputs:
- exchange: bfloat16 [32768, 32, 4, 256], P('row', None, 'aux')
Inputs may be any that keep to these rules, and one draw needn't show every extreme that they name: `tile_blocks`: each entry names a basis block at most 8 blocks away from its own row's block; the first slot of every block names the block itself. `screen_mask`: in every basis block the kept slots come first; some block keeps all 16.
All inputs are finite; a program needn't handle non-finite values.
Results may differ from a plain program's by a relative error of at most 0.0057.
Values may be sent and summed in bfloat16 or wider, within the bound.
No kernel may reach another device: no remote copies, remote signals or barrier semaphores. Data moves between devices by JAX's collectives and lax.ppermute only.
A program may use at most 128 MiB of HBM per device.

v0:
```python
import jax
import jax.numpy as jnp
from jax import lax
from jax.sharding import PartitionSpec as P


def with_halo(block, sides, width):
    for axis, dim in sides:
        count = lax.axis_size(axis)
        forward = [(i, i + 1) for i in range(count - 1)]
        backward = [(target, source) for source, target in forward]
        low = lax.ppermute(
            lax.slice_in_dim(block, block.shape[dim] - width, None, axis=dim), axis, forward
        )
        high = lax.ppermute(lax.slice_in_dim(block, 0, width, axis=dim), axis, backward)
        block = jnp.concatenate([low, block, high], axis=dim)
    return block


def per_device(b_tiles, occ_coeff, tile_blocks, screen_mask):
    p_local, rows_local, stored = b_tiles.shape
    blocks_local, slot_count = tile_blocks.shape
    block_size = rows_local // blocks_local
    orbitals = occ_coeff.shape[1]
    row_count = lax.axis_size("row")
    aux_count = lax.axis_size("aux")
    extended = with_halo(occ_coeff, (("row", 0),), rows_local)
    coeff_blocks = extended.reshape(3 * blocks_local, block_size, orbitals)
    local_index = tile_blocks - (lax.axis_index("row") - 1) * blocks_local
    picked = jnp.take(coeff_blocks, local_index, axis=0)
    keep_mask = screen_mask.astype(jnp.bfloat16)
    tiles_five = b_tiles.reshape(p_local, blocks_local, block_size, slot_count, block_size)
    masked = picked * keep_mask[:, :, None, None]
    half_sum = jnp.einsum(
        "pbmsn,bsni->pbmi", tiles_five, masked, preferred_element_type=jnp.float32
    )
    half_local = half_sum.astype(jnp.bfloat16).reshape(p_local, rows_local, orbitals)
    slab_rows = lax.all_gather(half_local, "aux", axis=0, tiled=True)
    share = rows_local // aux_count
    all_rows = lax.all_gather(half_local, "row", axis=1, tiled=True)
    split_rows = all_rows.reshape(p_local, row_count, aux_count, share, orbitals)
    regrouped = lax.all_to_all(split_rows, "aux", split_axis=2, concat_axis=0, tiled=True)
    partner = regrouped.reshape(p_local * aux_count, row_count * share, orbitals)
    result = jnp.einsum("pmi,pli->ml", slab_rows, partner, preferred_element_type=jnp.float32)
    return result.astype(jnp.bfloat16).reshape(rows_local, row_count, 1, share)


def solution(mesh):
    in_specs = (P("aux", "row", None), P("row", None), P("row", None), P("row", None))
    out_specs = P("row", None, "aux", None)
    return jax.shard_map(
        per_device, mesh=mesh, in_specs=in_specs, out_specs=out_specs, check_vma=False
    )
```

profile of v0, /device:TPU:1, one launch (start us, length us, event | category | flops | bytes accessed | tf_op | source)
XLA Modules:
  0.0 382.9 jit_solution(15495398956538830125)
XLA Ops:
  7.4 0.0 copy-start
  7.4 0.0 all-gather.5.cloned.1.call-start
  7.4 4.7 %collective-permute-start = (bf16[1024,256]{1,0:T(8,128)(2,1)}, bf16[1024,256]{1,0:T(8,128)(2,1)S(1)}, u32[]{:S(2)}, u32[]{:S(2)}) collective-permute-start(bf16[1024,256]{1,0:T(8,128)(2,1)} %param.5), channel_id=1, source_target_pairs={{0,1},{1,2},{2,3},{3,4},{4,5},{5,6},{6,7},{7,8},{8,9},{9,10},{10,1... | collective-permute-start | bytes 1572872 | tf_op jit(solution)/shard_map/ppermute | solution.py:12
  12.1 1.9 collective-permute-start.1
  14.0 0.7 compare_and_fusion
  14.7 0.1 reshape.37
  14.8 5.6 %copy.12 = bf16[128,8,16,128]{3,2,1,0:T(8,128)(2,1)} copy(bf16[128,8,16,128]{3,1,2,0:T(8,128)(2,1)} %bitcast.36) | data formatting | bytes 8388608
  20.4 0.0 copy-done.1
  20.4 0.0 collective-permute-done
  20.4 2.4 collective-permute-done.1
  22.8 0.0 copy-done
  22.8 0.1 pad_maximum_fusion
  22.9 6.7 %gather_fusion = bf16[128,128,256]{2,1,0:T(8,128)(2,1)} fusion(bf16[24,128,256]{2,1,0:T(8,128)(2,1)S(1)} %bitcast.32, s32[1024]{0:T(1024)S(1)} %pad_clamp_fusion), kind=kCustom, calls=%fused_computation | custom fusion | bytes 16777728 | tf_op jit(solution)/shard_map/jit(_take)/gather | solution.py:30
  29.7 8.2 %fusion.12 = bf16[8,256,128]{1,2,0:T(8,128)(2,1)} fusion(bf16[8,16,128,256]{3,2,1,0:T(8,128)(2,1)} %bitcast.35, pred[8,16]{1,0:T(8,128)(4,1)S(1)} %get-tuple-element.5, bf16[8,16]{1,0:T(8,128)(2,1)S(1)} %convert_element_type.15, bf16[8,128,16,128]{3,2,1,0:T(8,128)(2,1)} %bitcast.37), kind=kOutput, calls=%fused_computation.11 | convolution fusion | flops 1094975488 | bytes 13107584 | tf_op jit(solution)/shard_map/pbmsn,bsni->pbmi/dot_general | solution.py:34
  37.8 0.0 all-gather.5.cloned.1.call-update
  37.9 76.5 %all-gather.5.cloned.1.call-done = bf16[1,32768,256]{2,1,0:T(8,128)(2,1)} async-done(((bf16[1,1024,256]{2,1,0:T(8,128)(2,1)}), bf16[1,32768,256]{2,1,0:T(8,128)(2,1)}) %all-gather.5.cloned.1.call-update) | async-done | bytes 16777232 | tf_op jit(solution)/shard_map/all_gather | solution.py:40
  114.4 14.0 %copy.9 = bf16[1,32,4,256,256]{4,3,1,0,2:T(8,128)(2,1)} copy(bf16[1,32,4,256,256]{4,3,2,1,0:T(8,128)(2,1)} %bitcast.33) | data formatting | bytes 33554432 | tf_op jit(solution)/shard_map/reshape | solution.py:41
  128.3 7.0 %all-to-all-start = ((bf16[1,32,4,256,256]{4,3,1,0,2:T(8,128)(2,1)}), bf16[1,32,4,256,256]{4,3,1,0,2:T(8,128)(2,1)}, u32[]{:S(2)}, u32[]{:S(2)}) async-start(bf16[1,32,4,256,256]{4,3,1,0,2:T(8,128)(2,1)} %copy.9), calls=%async_computation | async-start | bytes 33554432 | tf_op jit(solution)/shard_map/all_to_all | solution.py:42
  135.3 0.0 all-gather.3.cloned.1.call-start
  135.4 0.5 all-gather.3.cloned.1.call-update
  135.9 48.8 %all-gather.3.cloned.1.call-done = bf16[4,1024,256]{2,1,0:T(8,128)(2,1)} async-done(((bf16[1,1024,256]{2,1,0:T(8,128)(2,1)}), bf16[4,1024,256]{2,1,0:T(8,128)(2,1)}) %all-gather.3.cloned.1.call-update) | async-done | bytes 2097168 | tf_op jit(solution)/shard_map/all_gather | solution.py:38
  184.8 151.0 %all-to-all-done = bf16[1,32,4,256,256]{4,3,1,0,2:T(8,128)(2,1)} async-done(((bf16[1,32,4,256,256]{4,3,1,0,2:T(8,128)(2,1)}), bf16[1,32,4,256,256]{4,3,1,0,2:T(8,128)(2,1)}, u32[]{:S(2)}, u32[]{:S(2)}) %all-to-all-start) | async-done | bytes 16777248 | tf_op jit(solution)/shard_map/all_to_all | solution.py:42
  335.8 24.1 %bitcast_convert_fusion = bf16[1024,8192]{1,0:T(8,128)(2,1)} fusion(bf16[4,1024,256]{2,1,0:T(8,128)(2,1)} %all-gather.3.cloned.1.call-done, bf16[4,8192,256]{2,1,0:T(8,128)(2,1)} %bitcast.12), kind=kOutput, calls=%fused_computation.1 | convolution fusion | flops 17188257792 | bytes 35651584 | tf_op jit(solution)/shard_map/pmi,pli->ml/dot_general | solution.py:44
  359.8 15.6 %copy.13 = bf16[128,8,32,256]{3,2,1,0:T(8,128)(2,1)} copy(bf16[128,8,32,256]{3,1,2,0:T(8,128)(2,1)} %bitcast.34) | data formatting | bytes 33554432
  (3 shorter events, 0.0 us)
Async XLA Ops:
  7.4 15.4 %copy-start = (bf16[1024,256]{1,0:T(8,128)(2,1)S(1)}, bf16[1024,256]{1,0:T(8,128)(2,1)}, u32[]{:S(2)}) copy-start(bf16[1024,256]{1,0:T(8,128)(2,1)} %param.5) | copy-start | bytes 1572868
  7.4 13.0 %copy-start.1 = (s32[8,16]{1,0:T(8,128)S(1)}, s32[8,16]{1,0:T(8,128)}, u32[]{:S(2)}) copy-start(s32[8,16]{1,0:T(8,128)} %param.7) | copy-start | bytes 1540
  7.4 107.0 %all-gather.5.cloned.1.call-start = ((), (), s32[]{:S(2)}) async-start(), calls=%async_computation.2 | async-start | bytes 17301504 | tf_op jit(solution)/shard_map/all_gather | solution.py:40
  7.4 13.0 %collective-permute-start = (bf16[1024,256]{1,0:T(8,128)(2,1)}, bf16[1024,256]{1,0:T(8,128)(2,1)S(1)}, u32[]{:S(2)}, u32[]{:S(2)}) collective-permute-start(bf16[1024,256]{1,0:T(8,128)(2,1)} %param.5), channel_id=1, source_target_pairs={{0,1},{1,2},{2,3},{3,4},{4,5},{5,6},{6,7},{7,8},{8,9},{9,10},{10,1... | collective-permute-start | bytes 1572872 | tf_op jit(solution)/shard_map/ppermute | solution.py:12
  12.1 10.7 %collective-permute-start.1 = (bf16[1024,256]{1,0:T(8,128)(2,1)}, bf16[1024,256]{1,0:T(8,128)(2,1)S(1)}, u32[]{:S(2)}, u32[]{:S(2)}) collective-permute-start(bf16[1024,256]{1,0:T(8,128)(2,1)} %param.5), channel_id=1, source_target_pairs={{1,0},{2,1},{3,2},{4,3},{5,4},{6,5},{7,6},{8,7},{9,8},{10,9},{11,1... | collective-permute-start | bytes 1572872 | tf_op jit(solution)/shard_map/ppermute | solution.py:15
  128.3 207.4 %all-to-all-start = ((bf16[1,32,4,256,256]{4,3,1,0,2:T(8,128)(2,1)}), bf16[1,32,4,256,256]{4,3,1,0,2:T(8,128)(2,1)}, u32[]{:S(2)}, u32[]{:S(2)}) async-start(bf16[1,32,4,256,256]{4,3,1,0,2:T(8,128)(2,1)} %copy.9), calls=%async_computation | async-start | bytes 33554432 | tf_op jit(solution)/shard_map/all_to_all | solution.py:42
  135.3 49.4 %all-gather.3.cloned.1.call-start = ((), (), s32[]{:S(2)}) async-start(), calls=%async_computation.1 | async-start | bytes 2621440 | tf_op jit(solution)/shard_map/all_gather | solution.py:38
Sparse Core Ops, SparseCore 0:
  38.0 76.3 all-gather.4
Sparse Core Ops, SparseCore 1:
  137.5 47.2 all-gather.2
where the time goes:
time: 383 us
  waiting for transfers between devices  279 us (73%)
  local copies, waits for them, and re-layouts  42 us (11%)
  matrix products  32.2 us (8%)
  between operations  14.9 us (4%)
  starting transfers between devices  13.7 us (4%)
    all_to_all x1, waiting for transfers between devices, per_device(): lax.all_to_all(split_rows, 'aux', split_axis=2, concat_axis=0, tiled=True)  151 us
    all_gather x1, waiting for transfers between devices, per_device(): all_rows = lax.all_gather(half_local, 'row', axis=1, tiled=True)  76.5 us
    all_gather x1, waiting for transfers between devices, per_device(): slab_rows = lax.all_gather(half_local, 'aux', axis=0, tiled=True)  48.8 us
    dot_general x1, matrix products, per_device(): jnp.einsum('pmi,pli->ml', slab_rows, partner, preferred_element_type=jnp....  24.1 us
    unnamed x6, local copies, waits for them, and re-layouts  21.2 us
    reshape x1, local copies, waits for them, and re-layouts, per_device(): all_rows.reshape(p_local, row_count, aux_count, share, orbitals)  14 us
    dot_general x1, matrix products, per_device(): jnp.einsum('pbmsn,bsni->pbmi', tiles_five, masked, preferred_element_type...  8.17 us
  transfers between devices with their start and end apart: 5, of which 4 were waited for; matrix products, arithmetic and copies ran while one was open for 2% of the time, Pallas kernels for 0%

commit v1 on v0

--- a/solution.py
+++ b/solution.py
@@ -37,7 +37,9 @@
     half_local = half_sum.astype(jnp.bfloat16).reshape(p_local, rows_local, orbitals)
     slab_rows = lax.all_gather(half_local, "aux", axis=0, tiled=True)
     share = rows_local // aux_count
-    all_rows = lax.all_gather(half_local, "row", axis=1, tiled=True)
+    all_rows = jnp.concatenate(
+        lax.all_to_all(jnp.stack([half_local] * lax.axis_size("row")), "row", 0, 0), axis=1
+    )
     split_rows = all_rows.reshape(p_local, row_count, aux_count, share, orbitals)
     regrouped = lax.all_to_all(split_rows, "aux", split_axis=2, concat_axis=0, tiled=True)
     partner = regrouped.reshape(p_local * aux_count, row_count * share, orbitals)

time: 383 us -> 494 us (1.29)
  blocking collectives: 0 us -> 195 us
  waiting for transfers between devices: 279 us -> 203 us
  local copies, waits for them, and re-layouts: 42 us -> 36.5 us
    all_to_all x0 -> x1, blocking collectives: none -> 195 us  [per_device(): lax.all_to_all(jnp.stack([half_local] * lax.axis_size('row')), 'row', 0, 0)]
    all_gather x1 -> x0, waiting for transfers between devices: 76.5 us -> none  [per_device(): all_rows = lax.all_gather(half_local, 'row', axis=1, tiled=True)]
    reshape x1 -> x0, local copies, waits for them, and re-layouts: 14 us -> none  [per_device(): all_rows.reshape(p_local, row_count, aux_count, share, orbitals)]
    another operation x0 -> x2, local copies, waits for them, and re-layouts: none -> 8.5 us  [the longest x1 6.53 us: per_device(): all_rows.reshape(p_local, row_count, aux_count, share, orbitals)]
    unnamed x6 -> x8, local copies, waits for them, and re-layouts: 21.2 us -> 21.2 us
  transfers between devices with their start and end apart: 5 -> 4, of which waited for: 4 -> 3; matrix products, arithmetic and copies ran while one was open for 2% -> 1% of each run, Pallas kernels for 0% -> 0%
where the time goes in v1:
time: 494 us
  waiting for transfers between devices  203 us (41%)
  blocking collectives  195 us (39%)
  local copies, waits for them, and re-layouts  36.5 us (7%)
  matrix products  31.4 us (6%)
  starting transfers between devices  13.7 us (3%)
  between operations  13.5 us (3%)
    all_to_all x1, blocking collectives, per_device(): lax.all_to_all(jnp.stack([half_local] * lax.axis_size('row')), 'row', 0, 0)  195 us
    all_to_all x1, waiting for transfers between devices, per_device(): lax.all_to_all(split_rows, 'aux', split_axis=2, concat_axis=0, tiled=True)  149 us
    all_gather x1, waiting for transfers between devices, per_device(): slab_rows = lax.all_gather(half_local, 'aux', axis=0, tiled=True)  50.8 us
    dot_general x1, matrix products, per_device(): jnp.einsum('pmi,pli->ml', slab_rows, partner, preferred_element_type=jnp....  24.1 us
    unnamed x8, local copies, waits for them, and re-layouts  21.2 us
  transfers between devices with their start and end apart: 4, of which 3 were waited for; matrix products, arithmetic and copies ran while one was open for 1% of the time, Pallas kernels for 0%

profile of v1, /device:TPU:1, one launch (start us, length us, event | category | flops | bytes accessed | tf_op | source)
XLA Modules:
  0.0 493.7 jit_solution(1522438948736765495)
XLA Ops:
  6.5 4.7 collective-permute-start
  11.3 1.9 collective-permute-start.1
  13.2 0.7 compare_and_fusion
  13.9 0.1 reshape.37
  14.0 5.6 %copy.14 = bf16[128,8,16,128]{3,2,1,0:T(8,128)(2,1)} copy(bf16[128,8,16,128]{3,1,2,0:T(8,128)(2,1)} %bitcast.38) | data formatting | bytes 8388608
  19.5 0.0 copy-done.2
  19.5 0.0 collective-permute-done
  19.6 2.4 collective-permute-done.1
  22.0 0.0 copy-done.1
  22.0 0.1 pad_maximum_fusion
  22.1 6.7 %gather_fusion = bf16[128,128,256]{2,1,0:T(8,128)(2,1)} fusion(bf16[24,128,256]{2,1,0:T(8,128)(2,1)S(1)} %bitcast.35, s32[1024]{0:T(1024)S(1)} %pad_clamp_fusion), kind=kCustom, calls=%fused_computation | custom fusion | bytes 16777728 | tf_op jit(solution)/shard_map/jit(_take)/gather | solution.py:30
  28.8 7.3 %fusion.12 = bf16[8,256,128]{1,2,0:T(8,128)(2,1)S(1)} fusion(bf16[8,16,128,256]{3,2,1,0:T(8,128)(2,1)} %bitcast.37, pred[8,16]{1,0:T(8,128)(4,1)S(1)} %get-tuple-element.5, bf16[8,16]{1,0:T(8,128)(2,1)S(1)} %convert_element_type.15, bf16[8,128,16,128]{3,2,1,0:T(8,128)(2,1)} %bitcast.39), kind=kOutput, calls=%fused_computation.11 | convolution fusion | flops 1094975488 | bytes 13107584 | tf_op jit(solution)/shard_map/pbmsn,bsni->pbmi/dot_general | solution.py:34
  36.2 0.0 copy-start
  36.2 2.0 stack.3
  38.2 0.0 copy-done
  38.2 195.2 %all_to_all.20 = bf16[32,1,1024,256]{3,2,1,0:T(8,128)(2,1)S(1)} all-to-all(bf16[32,1,1024,256]{3,2,1,0:T(8,128)(2,1)S(1)} %stack.3), channel_id=1, replica_groups=mesh['aux'=4,'row'=32] {'row'}, dimensions={0} | all-to-all | bytes 33554432 | tf_op jit(solution)/shard_map/all_to_all | solution.py:41
  233.4 6.5 %copy.11 = bf16[1,32,4,256,256]{4,3,1,0,2:T(8,128)(2,1)} copy(bf16[1,32,4,256,256]{4,3,2,1,0:T(8,128)(2,1)S(1)} %bitcast.34) | data formatting | bytes 33554432 | tf_op jit(solution)/shard_map/reshape;reshape | solution.py:43
  239.9 7.0 %all-to-all-start.1 = ((bf16[1,32,4,256,256]{4,3,1,0,2:T(8,128)(2,1)}), bf16[1,32,4,256,256]{4,3,1,0,2:T(8,128)(2,1)}, u32[]{:S(2)}, u32[]{:S(2)}) async-start(bf16[1,32,4,256,256]{4,3,1,0,2:T(8,128)(2,1)} %copy.11), calls=%async_computation.1 | async-start | bytes 33554432 | tf_op jit(solution)/shard_map/all_to_all | solution.py:44
  246.9 0.0 all-gather.2.cloned.1.call-start
  246.9 0.7 all-gather.2.cloned.1.call-update
  247.6 50.8 %all-gather.2.cloned.1.call-done = bf16[4,1024,256]{2,1,0:T(8,128)(2,1)} async-done(((bf16[1,1024,256]{2,1,0:T(8,128)(2,1)}), bf16[4,1024,256]{2,1,0:T(8,128)(2,1)}) %all-gather.2.cloned.1.call-update) | async-done | bytes 2097168 | tf_op jit(solution)/shard_map/all_gather | solution.py:38
  298.4 148.8 %all-to-all-done.1 = bf16[1,32,4,256,256]{4,3,1,0,2:T(8,128)(2,1)} async-done(((bf16[1,32,4,256,256]{4,3,1,0,2:T(8,128)(2,1)}), bf16[1,32,4,256,256]{4,3,1,0,2:T(8,128)(2,1)}, u32[]{:S(2)}, u32[]{:S(2)}) %all-to-all-start.1) | async-done | bytes 16777248 | tf_op jit(solution)/shard_map/all_to_all | solution.py:44
  447.1 24.1 %bitcast_convert_fusion = bf16[1024,8192]{1,0:T(8,128)(2,1)} fusion(bf16[4,1024,256]{2,1,0:T(8,128)(2,1)} %all-gather.2.cloned.1.call-done, bf16[4,8192,256]{2,1,0:T(8,128)(2,1)} %bitcast.12), kind=kOutput, calls=%fused_computation.1 | convolution fusion | flops 17188257792 | bytes 35651584 | tf_op jit(solution)/shard_map/pmi,pli->ml/dot_general | solution.py:46
  471.2 15.6 %copy.15 = bf16[128,8,32,256]{3,2,1,0:T(8,128)(2,1)} copy(bf16[128,8,32,256]{3,1,2,0:T(8,128)(2,1)} %bitcast.36) | data formatting | bytes 33554432
  (4 shorter events, 0.0 us)
Async XLA Ops:
  6.5 15.4 %copy-start.1 = (bf16[1024,256]{1,0:T(8,128)(2,1)S(1)}, bf16[1024,256]{1,0:T(8,128)(2,1)}, u32[]{:S(2)}) copy-start(bf16[1024,256]{1,0:T(8,128)(2,1)} %param.5) | copy-start | bytes 1572868
  6.5 13.0 %copy-start.2 = (s32[8,16]{1,0:T(8,128)S(1)}, s32[8,16]{1,0:T(8,128)}, u32[]{:S(2)}) copy-start(s32[8,16]{1,0:T(8,128)} %param.7) | copy-start | bytes 1540
  6.5 13.0 %collective-permute-start = (bf16[1024,256]{1,0:T(8,128)(2,1)}, bf16[1024,256]{1,0:T(8,128)(2,1)S(1)}, u32[]{:S(2)}, u32[]{:S(2)}) collective-permute-start(bf16[1024,256]{1,0:T(8,128)(2,1)} %param.5), channel_id=1, source_target_pairs={{0,1},{1,2},{2,3},{3,4},{4,5},{5,6},{6,7},{7,8},{8,9},{9,10},{10,1... | collective-permute-start | bytes 1572872 | tf_op jit(solution)/shard_map/ppermute | solution.py:12
  11.3 10.7 %collective-permute-start.1 = (bf16[1024,256]{1,0:T(8,128)(2,1)}, bf16[1024,256]{1,0:T(8,128)(2,1)S(1)}, u32[]{:S(2)}, u32[]{:S(2)}) collective-permute-start(bf16[1024,256]{1,0:T(8,128)(2,1)} %param.5), channel_id=1, source_target_pairs={{1,0},{2,1},{3,2},{4,3},{5,4},{6,5},{7,6},{8,7},{9,8},{10,9},{11,1... | collective-permute-start | bytes 1572872 | tf_op jit(solution)/shard_map/ppermute | solution.py:15
  36.2 2.0 copy-start
  239.9 207.3 %all-to-all-start.1 = ((bf16[1,32,4,256,256]{4,3,1,0,2:T(8,128)(2,1)}), bf16[1,32,4,256,256]{4,3,1,0,2:T(8,128)(2,1)}, u32[]{:S(2)}, u32[]{:S(2)}) async-start(bf16[1,32,4,256,256]{4,3,1,0,2:T(8,128)(2,1)} %copy.11), calls=%async_computation.1 | async-start | bytes 33554432 | tf_op jit(solution)/shard_map/all_to_all | solution.py:44
  246.9 51.5 %all-gather.2.cloned.1.call-start = ((), (), s32[]{:S(2)}) async-start(), calls=%async_computation.2 | async-start | bytes 2621440 | tf_op jit(solution)/shard_map/all_gather | solution.py:38
Sparse Core Ops, SparseCore 0:
  249.4 48.9 all-gather.1
